TPU v7x, 256 devices: a whole 4x4x8 slice. The times are simulated.
256 devices in a mesh: rep: 8 (over x, core), seq: 32 (over y, z).
Axes of the slice: x: 4, y: 4, z: 8, core: 2. Of those that a mesh axis runs over, the one named last changes fastest.
Arguments:
- tokens: bfloat16 [16, 256, 32, 1024], P('rep', 'seq'), may hold values from -250 to 250
- cotangent: bfloat16 [16, 256, 32, 1024], P('rep', 'seq'), may hold values from -6 to 6
- clip_counts: int32 [8], P('rep'), may hold values from 1 to 2, as said below
- windows: int32 [16, 4, 3], P('rep'), may hold values from 0 to 3, as said below
- window_counts: int32 [16, 4], P('rep'), may hold values from 1 to 3, as said below
- norm_gain: float32 [1024], replicated, may hold values from 0.5 to 4
- norm_bias: float32 [1024], replicated, may hold values from -3 to 3
- qkv_weight: bfloat16 [1024, 3072], replicated, may hold values from -0.5 to 0.5
- out_weight: bfloat16 [1024, 1024], replicated, may hold values from -0.1875 to 0.1875
Outputs:
- grad_input: bfloat16 [16, 256, 32, 1024], P('rep', 'seq')
- grad_qkv_weight: float32 [1024, 3072], P('seq')
- grad_out_weight: float32 [1024, 1024], P('seq')
- grad_gain: float32 [1024], P('seq')
- grad_bias: float32 [1024], P('seq')
Inputs may be any that keep to these rules, and one draw needn't show every extreme that they name: `clip_counts`: slots of a group at or past its count hold no clip; some group is full. `windows`: the first entry of each list is the window itself; the entries of a list are distinct. `window_counts`: some window of every clip uses all 3 entries.
All inputs are finite; a program needn't handle non-finite values.
Results may differ from a plain program's by a relative error of at most 0.025.
The roundings to bfloat16 on the way count: a program that leaves them out, or rounds other values in their place, can miss the bound.
Values may be sent and summed in bfloat16 or wider, within the bound.
No kernel may reach another device: no remote copies, remote signals or barrier semaphores. Data moves between devices by JAX's collectives and lax.ppermute only.
A program may use at most 128 MiB of HBM per device.

v0:
```python
from functools import partial
import math
import jax
import jax.numpy as jnp
from jax import lax
from jax.sharding import Mesh, PartitionSpec as P
import numpy as np

D = 1024
HEADS = 16
HEAD_DIM = 64
WIN = 64
MAXW = 3
NWIN = 4
EPSILON = 1e-05


def frame_mask(window_list, list_count, frame_count):
    used_slot = jnp.arange(MAXW)[None, :] < list_count[:, None]
    listed = (window_list[:, :, None] == jnp.arange(NWIN)[None, None, :]) & used_slot[:, :, None]
    allowed = jnp.any(listed, axis=1).astype(jnp.float32)
    member = (jnp.arange(frame_count)[:, None] // WIN == jnp.arange(NWIN)[None, :]).astype(
        jnp.float32
    )
    return jnp.dot(jnp.dot(member, allowed), member.T) > 0.5


def contract_rows(left_side, right_side):
    return lax.dot_general(
        left_side, right_side, (((0,), (0,)), ((), ())), preferred_element_type=jnp.float32
    )


def times_transpose(left_side, right_side):
    return lax.dot_general(
        left_side, right_side, (((1,), (1,)), ((), ())), preferred_element_type=jnp.float32
    )


def local(
    tokens,
    cotangent,
    clip_counts,
    windows,
    window_counts,
    norm_gain,
    norm_bias,
    qkv_weight,
    out_weight,
):
    seq_size = lax.axis_size(("y", "z"))
    rep_size = lax.axis_size(("x", "core"))
    clip_count = tokens.shape[0]
    live_slot = jnp.arange(clip_count) < clip_counts[0]
    grad_live = jnp.where(live_slot[:, None, None, None], cotangent, jnp.zeros_like(cotangent))
    gathered, grad_whole = (
        lax.all_to_all(tokens, ("y", "z"), split_axis=2, concat_axis=1, tiled=True),
        lax.all_to_all(grad_live, ("y", "z"), split_axis=2, concat_axis=1, tiled=True),
    )
    frame_count = gathered.shape[1]
    patch_count = gathered.shape[2]
    row_count = clip_count * frame_count * patch_count
    grad_scale = 1.0 / math.sqrt(clip_count * rep_size * frame_count * patch_count * seq_size)
    factor = HEAD_DIM ** (-0.5)
    head_shape = (clip_count, frame_count, patch_count, HEADS, HEAD_DIM)
    allowed = jax.vmap(partial(frame_mask, frame_count=frame_count))(windows, window_counts)[
        :, None, None
    ]
    flat_input = gathered.reshape(row_count, D).astype(jnp.float32)
    centred = flat_input - jnp.mean(flat_input, axis=1, keepdims=True)
    inv_std = lax.rsqrt(jnp.mean(centred * centred, axis=1, keepdims=True) + EPSILON)
    normal_hat = centred * inv_std
    normed = (normal_hat * norm_gain + norm_bias).astype(jnp.bfloat16)
    projected = jnp.dot(normed, qkv_weight, preferred_element_type=jnp.float32).astype(jnp.bfloat16)
    query_heads = projected[:, :D].reshape(head_shape)
    key_heads = projected[:, D : 2 * D].reshape(head_shape)
    value_heads = projected[:, 2 * D :].reshape(head_shape)
    scores = (
        jnp.einsum("cfphd,cgphd->cphfg", query_heads, key_heads, preferred_element_type=jnp.float32)
        * factor
    )
    row_max = jnp.max(jnp.where(allowed, scores, -1e30), axis=-1, keepdims=True)
    exp_scores = jnp.where(allowed, jnp.exp(scores - row_max), 0.0)
    attn_prob = exp_scores / jnp.sum(exp_scores, axis=-1, keepdims=True)
    prob_bf = attn_prob.astype(jnp.bfloat16)
    attended = jnp.einsum(
        "cphfg,cgphd->cfphd", prob_bf, value_heads, preferred_element_type=jnp.float32
    ).astype(jnp.bfloat16)
    attn_flat = attended.reshape(row_count, D)
    grad_flat = grad_whole.reshape(row_count, D)
    grad_attn = times_transpose(grad_flat, out_weight).astype(jnp.bfloat16).reshape(head_shape)
    grad_prob = jnp.einsum(
        "cfphd,cgphd->cphfg", grad_attn, value_heads, preferred_element_type=jnp.float32
    )
    grad_scores = (
        attn_prob * (grad_prob - jnp.sum(attn_prob * grad_prob, axis=-1, keepdims=True)) * factor
    ).astype(jnp.bfloat16)
    grad_query = jnp.einsum(
        "cphfg,cgphd->cfphd", grad_scores, key_heads, preferred_element_type=jnp.float32
    ).astype(jnp.bfloat16)
    grad_keys = jnp.einsum(
        "cphfg,cfphd->cgphd", grad_scores, query_heads, preferred_element_type=jnp.float32
    ).astype(jnp.bfloat16)
    grad_values = jnp.einsum(
        "cphfg,cfphd->cgphd", prob_bf, grad_attn, preferred_element_type=jnp.float32
    ).astype(jnp.bfloat16)
    grad_rows = jnp.concatenate(
        [
            grad_query.reshape(row_count, D),
            grad_keys.reshape(row_count, D),
            grad_values.reshape(row_count, D),
        ],
        axis=1,
    )
    grad_normed = times_transpose(grad_rows, qkv_weight)
    gain_term = jnp.sum(grad_normed * normal_hat, axis=0) * grad_scale
    bias_term = jnp.sum(grad_normed, axis=0) * grad_scale
    grad_hat = grad_normed * norm_gain
    grad_norm_in = (
        inv_std
        * (
            grad_hat
            - jnp.mean(grad_hat, axis=1, keepdims=True)
            - normal_hat * jnp.mean(grad_hat * normal_hat, axis=1, keepdims=True)
        )
    ).astype(jnp.bfloat16)
    returned = lax.all_to_all(
        grad_norm_in.reshape(clip_count, frame_count, patch_count, D),
        ("y", "z"),
        split_axis=1,
        concat_axis=2,
        tiled=True,
    )
    grad_input = (grad_live.astype(jnp.float32) + returned.astype(jnp.float32)).astype(jnp.bfloat16)
    seq_index = lax.axis_index(("y", "z"))
    side_terms = lax.psum(jnp.stack([gain_term, bias_term]), ("x", "core", "y", "z"))
    side_terms = lax.dynamic_slice_in_dim(
        side_terms, seq_index * (D // seq_size), D // seq_size, axis=1
    )
    upper_rows = contract_rows(normed, grad_rows)
    lower_rows = contract_rows(attn_flat, grad_flat)
    stacked = (jnp.concatenate([upper_rows, lower_rows], axis=1) * grad_scale).astype(jnp.bfloat16)
    x_size = lax.axis_size("x")
    width = stacked.shape[1] // (2 * x_size)
    split = stacked.reshape(D, x_size, 2, width)
    core = lax.axis_index("core")
    mine = lax.dynamic_index_in_dim(split, core, axis=2, keepdims=False)
    other = lax.dynamic_index_in_dim(split, 1 - core, axis=2, keepdims=False)
    got = lax.ppermute(other, "core", [(0, 1), (1, 0)])
    merged = (mine.astype(jnp.float32) + got.astype(jnp.float32)).astype(jnp.bfloat16)
    merged = lax.psum_scatter(merged, "y", scatter_dimension=0, tiled=True)
    merged = lax.psum_scatter(merged, "z", scatter_dimension=0, tiled=True)
    merged = lax.psum_scatter(merged, "x", scatter_dimension=1, tiled=True)
    summed = lax.all_gather(
        merged.reshape(merged.shape[0], width), ("x", "core"), axis=1, tiled=True
    ).astype(jnp.float32)
    return (grad_input, summed[:, : 3 * D], summed[:, 3 * D :], side_terms[0], side_terms[1])


def fine_mesh(mesh):
    devices = np.asarray(mesh.devices)
    rep_size, seq_size = devices.shape
    y_size = len({device.coords[1] for device in devices.flat})
    return Mesh(
        devices.reshape(rep_size // 2, 2, y_size, seq_size // y_size), ("x", "core", "y", "z")
    )


def solution(mesh):
    rep, seq = (("x", "core"), ("y", "z"))
    return jax.shard_map(
        local,
        mesh=fine_mesh(mesh),
        in_specs=(
            P(rep, seq, None, None),
            P(rep, seq, None, None),
            P(rep),
            P(rep, None, None),
            P(rep, None),
            P(),
            P(),
            P(),
            P(),
        ),
        out_specs=(P(rep, seq, None, None), P(seq, None), P(seq, None), P(seq), P(seq)),
        check_vma=False,
    )
```

profile of v0, /device:TPU:1, one launch (start us, length us, event | category | flops | bytes accessed | tf_op | source)
XLA Modules:
  0.0 401.1 jit_solution(5838071315834525960)
XLA Ops:
  7.2 2.9 copy.100
  10.1 12.0 %all-to-all-start = ((bf16[2,8,32,1024]{3,1,0,2:T(8,128)(2,1)}), bf16[2,8,32,1024]{3,1,0,2:T(8,128)(2,1)S(1)}, u32[]{:S(2)}, u32[]{:S(2)}) async-start(bf16[2,8,32,1024]{3,1,0,2:T(8,128)(2,1)} %copy.100), calls=%async_computation | async-start | bytes 2097152 | tf_op jit(solution)/shard_map/all_to_all | solution.py:57
  22.8 1.8 copy_select_fusion
  24.7 1.1 copy.114
  25.9 0.5 fusion.50
  26.4 0.3 copy.110
  26.6 20.4 %all-to-all-done = bf16[2,8,32,1024]{3,1,0,2:T(8,128)(2,1)S(1)} async-done(((bf16[2,8,32,1024]{3,1,0,2:T(8,128)(2,1)}), bf16[2,8,32,1024]{3,1,0,2:T(8,128)(2,1)S(1)}, u32[]{:S(2)}, u32[]{:S(2)}) %all-to-all-start) | async-done | bytes 1048608 | tf_op jit(solution)/shard_map/all_to_all | solution.py:57
  47.0 8.5 %all-to-all-start.1 = ((bf16[2,8,32,1024]{3,1,0,2:T(8,128)(2,1)}), bf16[2,8,32,1024]{3,1,0,2:T(8,128)(2,1)}, u32[]{:S(2)}, u32[]{:S(2)}) async-start(bf16[2,8,32,1024]{3,1,0,2:T(8,128)(2,1)} %copy.114), calls=%async_computation.1 | async-start | bytes 2097152 | tf_op jit(solution)/shard_map/all_to_all | solution.py:58
  55.9 1.6 convert_bitcast_fusion
  57.7 3.2 copy.105
  61.0 0.4 multiply_reduce_fusion.3
  61.7 2.0 add_convert_fusion
  63.7 6.9 %convolution_convert_fusion = bf16[512,3072]{1,0:T(8,128)(2,1)S(1)} fusion(bf16[512,1024]{1,0:T(8,128)(2,1)S(1)} %add_convert_fusion, bf16[1024,3072]{1,0:T(8,128)(2,1)} %param.16), kind=kOutput, calls=%fused_computation.13 | convolution fusion | flops 3222798336 | bytes 10485760 | tf_op jit(solution)/shard_map/dot_general | solution.py:74
  70.7 1.6 fusion.69
  72.3 2.4 reshape.255
  74.7 3.6 copy.120
  78.3 2.4 all-to-all-done.1
  80.7 1.3 copy.115
  82.0 1.0 copy-done.10
  83.0 1.3 convolution_convert_fusion.1
  84.3 1.3 reshape.257
  85.6 1.7 copy.118
  87.3 3.0 reshape.258
  90.3 2.5 copy.119
  92.8 2.9 reshape.256
  95.8 2.5 copy.112
  98.3 5.9 %fusion.71 = f32[2,16,256,256]{2,3,1,0:T(8,128)} fusion(bf16[2,256,16,64]{1,3,2,0:T(8,128)(2,1)S(1)} %copy.118, bf16[2,256,16,64]{1,3,2,0:T(8,128)(2,1)} %copy.119), kind=kOutput, calls=%fused_computation.88 | convolution fusion | flops 268435456 | bytes 10485760 | tf_op jit(solution)/shard_map/cfphd,cgphd->cphfg/dot_general | solution.py:92
  104.2 5.9 %fusion.70 = (f32[2,16,256]{2,1,0:T(8,128)S(1)}, f32[2,16,256,256]{2,3,1,0:T(8,128)}) fusion(pred[2,256,256]{1,2,0:T(8,128)(4,1)S(1)} %copy.110, bf16[2,256,16,64]{1,3,2,0:T(8,128)(2,1)S(1)} %copy-done.7, bf16[2,256,16,64]{1,3,2,0:T(8,128)(2,1)S(1)} %copy-done.6), kind=kOutput, calls=%fused_computation.87 | convolution fusion | flops 549454080 | bytes 10649600 | tf_op jit(solution)/shard_map/sub | solution.py:83
  110.0 14.1 %fusion.41 = bf16[2,256,1,16,64]{1,4,3,0,2:T(8,128)(2,1)} fusion(bf16[2,256,16,64]{1,3,2,0:T(8,128)(2,1)S(1)} %copy-done.6, f32[2,16,256,256]{2,3,1,0:T(8,128)} %fusion.71, f32[2,16,256,256]{2,3,1,0:T(8,128)} %get-tuple-element.32, f32[2,16,256]{2,1,0:T(8,128)S(1)} %get-tuple-element.31), kind=kOutput, calls=%fused_computation.43 | convolution fusion | flops 283648256 | bytes 18907136 | tf_op jit(solution)/shard_map/cphfg,cgphd->cfphd/dot_general | solution.py:98
  124.1 13.2 %fusion.38 = bf16[2,256,1,16,64]{1,4,3,0,2:T(8,128)(2,1)} fusion(bf16[2,256,16,64]{1,3,2,0:T(8,128)(2,1)S(1)} %copy-done.7, f32[2,16,256,256]{2,3,1,0:T(8,128)} %fusion.71, f32[2,16,256,256]{2,3,1,0:T(8,128)} %get-tuple-element.32, f32[2,16,256]{2,1,0:T(8,128)S(1)} %get-tuple-element.31), kind=kOutput, calls=%fused_computation.42 | convolution fusion | flops 283648256 | bytes 18907136 | tf_op jit(solution)/shard_map/cphfg,cfphd->cgphd/dot_general | solution.py:101
  137.3 4.9 %fusion.47 = bf16[2,256,1,16,64]{1,4,3,0,2:T(8,128)(2,1)S(1)} fusion(bf16[2,256,16,64]{1,3,2,0:T(8,128)(2,1)S(1)} %copy.118, f32[2,16,256,256]{2,3,1,0:T(8,128)} %get-tuple-element.32, f32[2,16,256]{2,1,0:T(8,128)S(1)} %get-tuple-element.31), kind=kOutput, calls=%fused_computation.45 | convolution fusion | flops 273154048 | bytes 10518528 | tf_op jit(solution)/shard_map/cphfg,cfphd->cgphd/dot_general | solution.py:104
  142.2 1.2 copy-done.19
  143.4 0.9 fusion.44
  144.3 0.3 copy-done.13
  144.6 1.1 copy.122
  146.0 1.1 copy.125
  147.3 1.1 copy.128
  148.7 1.1 copy.133
  150.0 1.3 fusion.73
  151.4 1.1 copy-done.9
  152.5 3.5 fusion.72
  156.0 4.4 %fusion.2 = bf16[1024,4096]{1,0:T(8,128)(2,1)} fusion(f32[1024,1024]{1,0:T(8,128)S(1)} %fusion.73, f32[1024,3072]{1,0:T(8,128)S(1)} %fusion.72), kind=kLoop, calls=%fused_computation.3 | loop fusion | flops 12582912 | bytes 25165824 | tf_op jit(solution)/shard_map/convert_element_type | solution.py:142
  160.4 14.4 %convert_element_type.146 = bf16[1024,4,2,512]{3,2,1,0:T(2,128)(2,1)} reshape(bf16[1024,4096]{1,0:T(8,128)(2,1)} %fusion.2) | data formatting | bytes 16777216 | tf_op jit(solution)/shard_map/convert_element_type | solution.py:142
  174.8 19.9 %constant_dynamic-slice_fusion.2 = (bf16[1024,4,1,512]{3,2,1,0:T(2,128)(2,1)S(1)}, bf16[1024,4,1,512]{3,2,1,0:T(2,128)(2,1)}) fusion(bf16[1024,4,2,512]{3,2,1,0:T(2,128)(2,1)} %convert_element_type.146, s32[]{:T(128)S(6)} %select_n.39, s32[]{:T(128)S(6)} %select_n.40), kind=kLoop, calls=%fused_computation.76 | loop fusion | bytes 16777224 | tf_op jit(solution)/shard_map/jit(dynamic_index_in_dim)/dynamic_slice | solution.py:147
  194.7 5.8 %copy.167 = bf16[1024,4,1,512]{3,0,1,2:T(8,128)(2,1)S(1)} copy(bf16[1024,4,1,512]{3,2,1,0:T(2,128)(2,1)} %get-tuple-element.25) | data formatting | bytes 8388608 | tf_op jit(solution)/shard_map/jit(dynamic_index_in_dim)/dynamic_slice | solution.py:148
  200.5 4.6 %collective-permute-start = (bf16[1024,4,512]{2,0,1:T(8,128)(2,1)S(1)}, bf16[1024,4,512]{2,0,1:T(8,128)(2,1)S(1)}, u32[]{:S(2)}, u32[]{:S(2)}) collective-permute-start(bf16[1024,4,512]{2,0,1:T(8,128)(2,1)S(1)} %bitcast.120), channel_id=1, source_target_pairs={{0,32},{32,0},{1,33},{33,1},{2,34},{34,2},{3,35},{35,3},{4,36},{36... | collective-permute-start | bytes 12582920 | tf_op jit(solution)/shard_map/ppermute | solution.py:149
  205.1 6.8 %collective-permute-done = bf16[1024,4,512]{2,0,1:T(8,128)(2,1)S(1)} collective-permute-done((bf16[1024,4,512]{2,0,1:T(8,128)(2,1)S(1)}, bf16[1024,4,512]{2,0,1:T(8,128)(2,1)S(1)}, u32[]{:S(2)}, u32[]{:S(2)}) %collective-permute-start) | collective-permute-done | bytes 4194336 | tf_op jit(solution)/shard_map/ppermute | solution.py:149
  211.9 2.0 copy-done.5
  213.9 6.7 %fusion.3 = bf16[1024,4,512]{2,0,1:T(8,128)(2,1)} fusion(bf16[1024,4,512]{2,0,1:T(8,128)(2,1)} %copy-done.5, bf16[1024,4,1,512]{3,2,1,0:T(2,128)(2,1)S(1)} %get-tuple-element.24), kind=kLoop, calls=%fused_computation.5 | loop fusion | flops 8388608 | bytes 12582912 | tf_op jit(solution)/shard_map/convert_element_type | solution.py:150
  220.6 0.3 reduce-scatter.6.cloned.1.call-start
  221.0 1.3 copy-done.2
  222.2 9.0 %multiply_reduce_fusion.1 = (f32[1024]{0:T(1024)S(1)}, f32[512]{0:T(512)S(1)}, f32[512]{0:T(512)S(1)}, f32[1024]{0:T(1024)S(1)}, f32[512,1024]{1,0:T(8,128)}) fusion(f32[2,32,8,1,1024]{4,2,1,0,3:T(8,128)S(1)} %copy-done.2, f32[512]{0:T(512)S(1)} %div.35, f32[512]{0:T(512)S(1)} %rsqrt.12, f32[1024]{0:T(1024)S(1)} %copy-done.15, ...), kind=kOutput, calls=%fused_computation.27 | convolution fusion | flops 3225940992 | bytes 13651968 | tf_op jit(solution)/shard_map/dot_general | solution.py:35
  231.2 35.0 %reduce-scatter.4.cloned.1.call-done = bf16[256,4,512]{2,0,1:T(8,128)(2,1)} async-done(((bf16[1024,4,512]{2,0,1:T(8,128)(2,1)}), bf16[256,4,512]{2,0,1:T(8,128)(2,1)}) %reduce-scatter.4.cloned.1.call-update) | async-done | bytes 1048592 | tf_op jit(solution)/shard_map/reduce_scatter | solution.py:151
  266.3 2.3 multiply_convert_fusion.1
  268.6 2.0 copy.129
  270.6 8.2 %all-to-all-start.2 = ((bf16[2,256,1,1024]{3,0,2,1:T(2,128)(2,1)}), bf16[2,256,1,1024]{3,0,2,1:T(2,128)(2,1)}, u32[]{:S(2)}, u32[]{:S(2)}) async-start(bf16[2,256,1,1024]{3,0,2,1:T(2,128)(2,1)} %copy.129), calls=%async_computation.2 | async-start | bytes 2097152 | tf_op jit(solution)/shard_map/all_to_all | solution.py:127
  278.9 78.9 %psum.7 = f32[2,1024]{1,0:T(2,128)S(1)} all-reduce(f32[2,1024]{1,0:T(2,128)S(1)} %pad_maximum_fusion), channel_id=1, replica_groups=mesh['x'=4,'core'=2,'y'=4,'z'=8] {'x','core','y','z'}, use_global_device_ids=true, to_apply=%region_13.14 | all-reduce | flops 2048 | bytes 16384 | tf_op jit(solution)/shard_map/psum | solution.py:136
  357.9 0.5 slice_bitcast_fusion
  358.5 2.0 fusion.20
  360.5 1.5 copy.137
  362.0 14.8 %reduce-scatter.8.cloned.1.call-done = bf16[32,1,512]{2,0,1:T(8,128)(2,1)} async-done(((bf16[32,4,512]{2,0,1:T(8,128)(2,1)}), bf16[32,1,512]{2,0,1:T(8,128)(2,1)}) %reduce-scatter.8.cloned.1.call-update) | async-done | bytes 32784 | tf_op jit(solution)/shard_map/reduce_scatter | solution.py:153
  376.8 15.8 %all-gather = bf16[32,1,4096]{2,0,1:T(8,128)(2,1)S(1)} all-gather(bf16[32,1,512]{2,0,1:T(8,128)(2,1)} %reduce-scatter.8.cloned.1.call-done), channel_id=2, replica_groups=mesh['x'=4,'core'=2,'y'=4,'z'=8] {'x','core'}, dimensions={2}, use_global_device_ids=true | all-gather | bytes 294912 | tf_op jit(solution)/shard_map/all_gather | solution.py:154
  392.7 0.8 slice.31
  393.4 0.7 slice.32
  (68 shorter events, 2.4 us)
Async XLA Ops:
  7.2 75.8 %copy-start = (bf16[1024,1024]{1,0:T(8,128)(2,1)S(1)}, bf16[1024,1024]{1,0:T(8,128)(2,1)}, u32[]{:S(2)}) copy-start(bf16[1024,1024]{1,0:T(8,128)(2,1)} %param.17) | copy-start | bytes 6291460
  7.2 18.6 %copy-start.17 = (s32[2,4,3]{1,0,2:T(2,128)S(1)}, s32[2,4,3]{1,0,2:T(2,128)}, u32[]{:S(2)}) copy-start(s32[2,4,3]{1,0,2:T(2,128)} %param.12) | copy-start | bytes 292
  7.2 18.6 %copy-start.18 = (s32[2,4]{1,0:T(2,128)S(1)}, s32[2,4]{1,0:T(2,128)}, u32[]{:S(2)}) copy-start(s32[2,4]{1,0:T(2,128)} %param.13) | copy-start | bytes 100
  10.1 36.9 %all-to-all-start = ((bf16[2,8,32,1024]{3,1,0,2:T(8,128)(2,1)}), bf16[2,8,32,1024]{3,1,0,2:T(8,128)(2,1)S(1)}, u32[]{:S(2)}, u32[]{:S(2)}) async-start(bf16[2,8,32,1024]{3,1,0,2:T(8,128)(2,1)} %copy.100), calls=%async_computation | async-start | bytes 2097152 | tf_op jit(solution)/shard_map/all_to_all | solution.py:57
  47.0 33.6 %all-to-all-start.1 = ((bf16[2,8,32,1024]{3,1,0,2:T(8,128)(2,1)}), bf16[2,8,32,1024]{3,1,0,2:T(8,128)(2,1)}, u32[]{:S(2)}, u32[]{:S(2)}) async-start(bf16[2,8,32,1024]{3,1,0,2:T(8,128)(2,1)} %copy.114), calls=%async_computation.1 | async-start | bytes 2097152 | tf_op jit(solution)/shard_map/all_to_all | solution.py:58
  55.5 210.8 %reduce-scatter.4.cloned.1.call-start = ((), (), s32[]{:S(2)}) async-start(), calls=%async_computation.6 | async-start | bytes 5242880 | tf_op jit(solution)/shard_map/reduce_scatter | solution.py:151
  55.9 5.8 %copy-start.15 = (f32[1024]{0:T(1024)S(1)}, f32[1024]{0:T(1024)}, u32[]{:S(2)}) copy-start(f32[1024]{0:T(1024)} %param.14) | copy-start | bytes 12292
  55.9 5.8 %copy-start.16 = (f32[1024]{0:T(1024)S(1)}, f32[1024]{0:T(1024)}, u32[]{:S(2)}) copy-start(f32[1024]{0:T(1024)} %param.15) | copy-start | bytes 12292
  63.7 7.0 %copy-start.8 = (bf16[512,1024]{1,0:T(8,128)(2,1)}, bf16[512,1024]{1,0:T(8,128)(2,1)S(1)}, u32[]{:S(2)}) copy-start(bf16[512,1024]{1,0:T(8,128)(2,1)S(1)} %add_convert_fusion) | copy-start | bytes 3145732
  82.0 1.0 copy-start.10
  98.3 5.9 %copy-start.6 = (bf16[2,256,16,64]{1,3,2,0:T(8,128)(2,1)S(1)}, bf16[2,256,16,64]{1,3,2,0:T(8,128)(2,1)}, u32[]{:S(2)}) copy-start(bf16[2,256,16,64]{1,3,2,0:T(8,128)(2,1)} %copy.120) | copy-start | bytes 3145732
  98.3 5.9 %copy-start.7 = (bf16[2,256,16,64]{1,3,2,0:T(8,128)(2,1)S(1)}, bf16[2,256,16,64]{1,3,2,0:T(8,128)(2,1)}, u32[]{:S(2)}) copy-start(bf16[2,256,16,64]{1,3,2,0:T(8,128)(2,1)} %copy.112) | copy-start | bytes 3145732
  137.3 4.9 %copy-start.3 = (bf16[2,256,16,64]{1,3,2,0:T(8,128)(2,1)S(1)}, bf16[2,256,16,64]{1,3,2,0:T(8,128)(2,1)}, u32[]{:S(2)}) copy-start(bf16[2,256,16,64]{1,3,2,0:T(8,128)(2,1)} %copy.119) | copy-start | bytes 3145732
  137.3 6.1 %copy-start.19 = (f32[2,16,256,256]{2,3,1,0:T(8,128)S(1)}, f32[2,16,256,256]{2,3,1,0:T(8,128)}, u32[]{:S(2)}) copy-start(f32[2,16,256,256]{2,3,1,0:T(8,128)} %get-tuple-element.32) | copy-start | bytes 25165828
  143.4 1.2 copy-start.13
  144.6 1.4 copy-start.12
  147.3 2.7 copy-start.11
  151.3 1.2 copy-start.9
  152.5 3.5 copy-start.14
  200.5 11.4 %collective-permute-start = (bf16[1024,4,512]{2,0,1:T(8,128)(2,1)S(1)}, bf16[1024,4,512]{2,0,1:T(8,128)(2,1)S(1)}, u32[]{:S(2)}, u32[]{:S(2)}) collective-permute-start(bf16[1024,4,512]{2,0,1:T(8,128)(2,1)S(1)} %bitcast.120), channel_id=1, source_target_pairs={{0,32},{32,0},{1,33},{33,1},{2,34},{34,2},{3,35},{35,3},{4,36},{36... | collective-permute-start | bytes 12582920 | tf_op jit(solution)/shard_map/ppermute | solution.py:149
  211.9 2.0 copy-start.5
  220.6 1.6 copy-start.2
  220.6 137.8 %reduce-scatter.6.cloned.1.call-start = ((), (), s32[]{:S(2)}) async-start(), calls=%async_computation.7 | async-start | bytes 1179648 | tf_op jit(solution)/shard_map/reduce_scatter | solution.py:152
  266.3 92.2 %copy-start.4 = (bf16[2,8,32,1024]{3,2,1,0:T(8,128)(2,1)S(1)}, bf16[2,8,32,1024]{3,2,1,0:T(8,128)(2,1)}, u32[]{:S(2)}) copy-start(bf16[2,8,32,1024]{3,2,1,0:T(8,128)(2,1)} %param.10) | copy-start | bytes 3145732
  270.6 87.8 %all-to-all-start.2 = ((bf16[2,256,1,1024]{3,0,2,1:T(2,128)(2,1)}), bf16[2,256,1,1024]{3,0,2,1:T(2,128)(2,1)}, u32[]{:S(2)}, u32[]{:S(2)}) async-start(bf16[2,256,1,1024]{3,0,2,1:T(2,128)(2,1)} %copy.129), calls=%async_computation.2 | async-start | bytes 2097152 | tf_op jit(solution)/shard_map/all_to_all | solution.py:127
  278.8 115.3 %copy-start.1 = (bf16[1024,1024]{1,0:T(8,128)(2,1)S(1)}, bf16[1024,1024]{1,0:T(8,128)(2,1)}, u32[]{:S(2)}) copy-start(bf16[1024,1024]{1,0:T(8,128)(2,1)} %param.17) | copy-start | bytes 6291460
  278.8 98.0 %reduce-scatter.8.cloned.1.call-start = ((), (), s32[]{:S(2)}) async-start(), calls=%async_computation.8 | async-start | bytes 163840 | tf_op jit(solution)/shard_map/reduce_scatter | solution.py:153
Sparse Core Ops, SparseCore 0:
  220.8 45.4 reduce-scatter.3
  268.8 46.9 reduce-scatter.5
  358.6 18.1 reduce-scatter.7
where the time goes:
time: 406 us; the launch traced here: 401 us
  blocking collectives  94.7 us (23%)
  local copies, waits for them, and re-layouts  89 us (22%)
  waiting for transfers between devices  79.4 us (20%)
  matrix products  67.3 us (17%)
  starting transfers between devices  33.7 us (8%)
  other arithmetic  21.7 us (5%)
  between operations  15.3 us (4%)
    psum x1, blocking collectives, local(): lax.psum(jnp.stack([gain_term, bias_term]), ('x', 'core', 'y', 'z'))  78.9 us
    reduce_scatter x1, waiting for transfers between devices, local(): merged = lax.psum_scatter(merged, 'y', scatter_dimension=0, tiled=True)  35 us
    all_to_all x1, waiting for transfers between devices, local(): lax.all_to_all(tokens, ('y', 'z'), split_axis=2, concat_axis=1, tiled=True)  20.4 us
    dynamic_slice x1, local copies, waits for them, and re-layouts, local(): mine = lax.dynamic_index_in_dim(split, core, axis=2, keepdims=False)  19.9 us
    another operation x8, local copies, waits for them, and re-layouts  19.9 us
    all_gather x1, blocking collectives, local(): lax.all_gather(merged.reshape(merged.shape[0], width), ('x', 'core'), axi...  15.8 us
    reduce_scatter x1, waiting for transfers between devices, local(): merged = lax.psum_scatter(merged, 'x', scatter_dimension=1, tiled=True)  14.8 us
    convert_element_type x1, local copies, waits for them, and re-layouts, local(): (jnp.concatenate([upper_rows, lower_rows], axis=1) * grad_scale).astype(j...  14.4 us
  transfers between devices with their start and end apart: 7, of which 5 were waited for; matrix products, arithmetic and copies ran while one was open for 11% of the time, Pallas kernels for 0%

commit v1 on v0

--- a/solution.py
+++ b/solution.py
@@ -13,6 +13,12 @@
 MAXW = 3
 NWIN = 4
 EPSILON = 1e-05
+
+
+def summed_here(array, name):
+    parts = lax.all_gather(array, name, axis=0, tiled=False)
+    total = parts.sum(axis=0)
+    return total
 
 
 def frame_mask(window_list, list_count, frame_count):
@@ -133,7 +139,7 @@
     )
     grad_input = (grad_live.astype(jnp.float32) + returned.astype(jnp.float32)).astype(jnp.bfloat16)
     seq_index = lax.axis_index(("y", "z"))
-    side_terms = lax.psum(jnp.stack([gain_term, bias_term]), ("x", "core", "y", "z"))
+    side_terms = summed_here(jnp.stack([gain_term, bias_term]), ("x", "core", "y", "z"))
     side_terms = lax.dynamic_slice_in_dim(
         side_terms, seq_index * (D // seq_size), D // seq_size, axis=1
     )

time: 406 us -> 408 us (level)
  waiting for transfers between devices: 79.4 us -> 159 us
  blocking collectives: 94.7 us -> 15.8 us
    psum x1 -> x0, blocking collectives: 78.9 us -> none  [local(): lax.psum(jnp.stack([gain_term, bias_term]), ('x', 'core', 'y', 'z'))]
    all_gather x0 -> x1, waiting for transfers between devices: none -> 74.1 us  [summed_here(): parts = lax.all_gather(array, name, axis=0, tiled=False)]
    reduce_scatter x1, waiting for transfers between devices: 14.8 us -> 19.1 us  [local(): merged = lax.psum_scatter(merged, 'x', scatter_dimension=1, tiled=True)]
  transfers between devices with their start and end apart: 7 -> 8, of which waited for: 5 -> 6; matrix products, arithmetic and copies ran while one was open for 11% -> 12% of each run, Pallas kernels for 0% -> 0%
where the time goes in v1:
time: 408 us; the launch traced here: 403 us
  waiting for transfers between devices  159 us (39%)
  local copies, waits for them, and re-layouts  88.9 us (22%)
  matrix products  67.3 us (16%)
  starting transfers between devices  30.4 us (7%)
  other arithmetic  24.6 us (6%)
  between operations  16.7 us (4%)
  blocking collectives  15.8 us (4%)
    all_gather x1, waiting for transfers between devices, summed_here(): parts = lax.all_gather(array, name, axis=0, tiled=False)  74.1 us
    reduce_scatter x1, waiting for transfers between devices, local(): merged = lax.psum_scatter(merged, 'y', scatter_dimension=0, tiled=True)  36.5 us
    all_to_all x1, waiting for transfers between devices, local(): lax.all_to_all(tokens, ('y', 'z'), split_axis=2, concat_axis=1, tiled=True)  20.4 us
    dynamic_slice x1, local copies, waits for them, and re-layouts, local(): mine = lax.dynamic_index_in_dim(split, core, axis=2, keepdims=False)  20 us
    another operation x8, local copies, waits for them, and re-layouts  19.9 us
    reduce_scatter x1, waiting for transfers between devices, local(): merged = lax.psum_scatter(merged, 'x', scatter_dimension=1, tiled=True)  19.1 us
    all_gather x1, blocking collectives, local(): lax.all_gather(merged.reshape(merged.shape[0], width), ('x', 'core'), axi...  15.8 us
    convert_element_type x1, local copies, waits for them, and re-layouts, local(): (jnp.concatenate([upper_rows, lower_rows], axis=1) * grad_scale).astype(j...  14.4 us
  transfers between devices with their start and end apart: 8, of which 6 were waited for; matrix products, arithmetic and copies ran while one was open for 12% of the time, Pallas kernels for 0%

profile of v1, /device:TPU:1, one launch (start us, length us, event | category | flops | bytes accessed | tf_op | source)
XLA Modules:
  0.0 403.1 jit_solution(11173302674513016705)
XLA Ops:
  8.0 2.9 copy.100
  11.0 12.0 %all-to-all-start = ((bf16[2,8,32,1024]{3,1,0,2:T(8,128)(2,1)}), bf16[2,8,32,1024]{3,1,0,2:T(8,128)(2,1)S(1)}, u32[]{:S(2)}, u32[]{:S(2)}) async-start(bf16[2,8,32,1024]{3,1,0,2:T(8,128)(2,1)} %copy.100), calls=%async_computation | async-start | bytes 2097152 | tf_op jit(solution)/shard_map/all_to_all | solution.py:63
  23.6 1.8 copy_select_fusion
  25.5 1.1 copy.114
  26.7 0.5 fusion.50
  27.5 20.4 %all-to-all-done = bf16[2,8,32,1024]{3,1,0,2:T(8,128)(2,1)S(1)} async-done(((bf16[2,8,32,1024]{3,1,0,2:T(8,128)(2,1)}), bf16[2,8,32,1024]{3,1,0,2:T(8,128)(2,1)S(1)}, u32[]{:S(2)}, u32[]{:S(2)}) %all-to-all-start) | async-done | bytes 1048608 | tf_op jit(solution)/shard_map/all_to_all | solution.py:63
  47.9 8.5 %all-to-all-start.1 = ((bf16[2,8,32,1024]{3,1,0,2:T(8,128)(2,1)}), bf16[2,8,32,1024]{3,1,0,2:T(8,128)(2,1)}, u32[]{:S(2)}, u32[]{:S(2)}) async-start(bf16[2,8,32,1024]{3,1,0,2:T(8,128)(2,1)} %copy.114), calls=%async_computation.1 | async-start | bytes 2097152 | tf_op jit(solution)/shard_map/all_to_all | solution.py:64
  56.7 1.6 convert_bitcast_fusion
  58.5 3.2 copy.105
  61.8 0.4 multiply_reduce_fusion.3
  62.5 2.0 add_convert_fusion
  64.5 7.0 %convolution_convert_fusion = bf16[512,3072]{1,0:T(8,128)(2,1)S(1)} fusion(bf16[512,1024]{1,0:T(8,128)(2,1)S(1)} %add_convert_fusion, bf16[1024,3072]{1,0:T(8,128)(2,1)} %param.16), kind=kOutput, calls=%fused_computation.13 | convolution fusion | flops 3222798336 | bytes 10485760 | tf_op jit(solution)/shard_map/dot_general | solution.py:80
  71.5 1.6 fusion.69
  73.1 2.3 reshape.259
  75.5 3.6 copy.120
  79.1 2.4 all-to-all-done.1
  81.5 1.3 copy.115
  82.8 1.0 copy-done.10
  83.8 1.3 convolution_convert_fusion.1
  85.1 1.3 reshape.261
  86.5 1.7 copy.118
  88.1 3.0 reshape.262
  91.1 2.5 copy.119
  93.6 2.9 reshape.260
  96.6 2.5 copy.112
  99.1 5.9 %fusion.71 = f32[2,16,256,256]{2,3,1,0:T(8,128)} fusion(bf16[2,256,16,64]{1,3,2,0:T(8,128)(2,1)S(1)} %copy.118, bf16[2,256,16,64]{1,3,2,0:T(8,128)(2,1)} %copy.119), kind=kOutput, calls=%fused_computation.88 | convolution fusion | flops 268435456 | bytes 10485760 | tf_op jit(solution)/shard_map/cfphd,cgphd->cphfg/dot_general | solution.py:98
  105.0 5.9 %fusion.70 = (f32[2,16,256]{2,1,0:T(8,128)S(1)}, f32[2,16,256,256]{2,3,1,0:T(8,128)}) fusion(pred[2,256,256]{1,2,0:T(8,128)(4,1)S(1)} %copy.110, bf16[2,256,16,64]{1,3,2,0:T(8,128)(2,1)S(1)} %copy-done.7, bf16[2,256,16,64]{1,3,2,0:T(8,128)(2,1)S(1)} %copy-done.6), kind=kOutput, calls=%fused_computation.87 | convolution fusion | flops 549454080 | bytes 10649600 | tf_op jit(solution)/shard_map/sub | solution.py:89
  110.8 14.1 %fusion.41 = bf16[2,256,1,16,64]{1,4,3,0,2:T(8,128)(2,1)} fusion(bf16[2,256,16,64]{1,3,2,0:T(8,128)(2,1)S(1)} %copy-done.6, f32[2,16,256,256]{2,3,1,0:T(8,128)} %fusion.71, f32[2,16,256,256]{2,3,1,0:T(8,128)} %get-tuple-element.32, f32[2,16,256]{2,1,0:T(8,128)S(1)} %get-tuple-element.31), kind=kOutput, calls=%fused_computation.43 | convolution fusion | flops 283648256 | bytes 18907136 | tf_op jit(solution)/shard_map/cphfg,cgphd->cfphd/dot_general | solution.py:104
  124.9 13.2 %fusion.38 = bf16[2,256,1,16,64]{1,4,3,0,2:T(8,128)(2,1)} fusion(bf16[2,256,16,64]{1,3,2,0:T(8,128)(2,1)S(1)} %copy-done.7, f32[2,16,256,256]{2,3,1,0:T(8,128)} %fusion.71, f32[2,16,256,256]{2,3,1,0:T(8,128)} %get-tuple-element.32, f32[2,16,256]{2,1,0:T(8,128)S(1)} %get-tuple-element.31), kind=kOutput, calls=%fused_computation.42 | convolution fusion | flops 283648256 | bytes 18907136 | tf_op jit(solution)/shard_map/cphfg,cfphd->cgphd/dot_general | solution.py:107
  138.0 4.9 %fusion.47 = bf16[2,256,1,16,64]{1,4,3,0,2:T(8,128)(2,1)S(1)} fusion(bf16[2,256,16,64]{1,3,2,0:T(8,128)(2,1)S(1)} %copy.118, f32[2,16,256,256]{2,3,1,0:T(8,128)} %get-tuple-element.32, f32[2,16,256]{2,1,0:T(8,128)S(1)} %get-tuple-element.31), kind=kOutput, calls=%fused_computation.45 | convolution fusion | flops 273154048 | bytes 10518528 | tf_op jit(solution)/shard_map/cphfg,cfphd->cgphd/dot_general | solution.py:110
  143.0 1.2 copy-done.19
  144.1 0.9 fusion.44
  145.4 1.1 copy.122
  146.8 1.1 copy.125
  148.1 1.1 copy.128
  149.4 1.1 copy.133
  150.8 1.3 fusion.73
  152.2 1.1 copy-done.9
  153.3 3.5 fusion.72
  156.8 4.3 %fusion.2 = bf16[1024,4096]{1,0:T(8,128)(2,1)} fusion(f32[1024,1024]{1,0:T(8,128)S(1)} %fusion.73, f32[1024,3072]{1,0:T(8,128)S(1)} %fusion.72), kind=kLoop, calls=%fused_computation.3 | loop fusion | flops 12582912 | bytes 25165824 | tf_op jit(solution)/shard_map/convert_element_type | solution.py:148
  161.1 14.4 %convert_element_type.146 = bf16[1024,4,2,512]{3,2,1,0:T(2,128)(2,1)} reshape(bf16[1024,4096]{1,0:T(8,128)(2,1)} %fusion.2) | data formatting | bytes 16777216 | tf_op jit(solution)/shard_map/convert_element_type | solution.py:148
  175.5 20.0 %constant_dynamic-slice_fusion.2 = (bf16[1024,4,1,512]{3,2,1,0:T(2,128)(2,1)S(1)}, bf16[1024,4,1,512]{3,2,1,0:T(2,128)(2,1)}) fusion(bf16[1024,4,2,512]{3,2,1,0:T(2,128)(2,1)} %convert_element_type.146, s32[]{:T(128)S(6)} %select_n.39, s32[]{:T(128)S(6)} %select_n.40), kind=kLoop, calls=%fused_computation.76 | loop fusion | bytes 16777224 | tf_op jit(solution)/shard_map/jit(dynamic_index_in_dim)/dynamic_slice | solution.py:153
  195.5 5.8 %copy.167 = bf16[1024,4,1,512]{3,0,1,2:T(8,128)(2,1)S(1)} copy(bf16[1024,4,1,512]{3,2,1,0:T(2,128)(2,1)} %get-tuple-element.25) | data formatting | bytes 8388608 | tf_op jit(solution)/shard_map/jit(dynamic_index_in_dim)/dynamic_slice | solution.py:154
  201.3 4.6 %collective-permute-start = (bf16[1024,4,512]{2,0,1:T(8,128)(2,1)S(1)}, bf16[1024,4,512]{2,0,1:T(8,128)(2,1)S(1)}, u32[]{:S(2)}, u32[]{:S(2)}) collective-permute-start(bf16[1024,4,512]{2,0,1:T(8,128)(2,1)S(1)} %bitcast.122), channel_id=1, source_target_pairs={{0,32},{32,0},{1,33},{33,1},{2,34},{34,2},{3,35},{35,3},{4,36},{36... | collective-permute-start | bytes 12582920 | tf_op jit(solution)/shard_map/ppermute | solution.py:155
  205.9 6.8 %collective-permute-done = bf16[1024,4,512]{2,0,1:T(8,128)(2,1)S(1)} collective-permute-done((bf16[1024,4,512]{2,0,1:T(8,128)(2,1)S(1)}, bf16[1024,4,512]{2,0,1:T(8,128)(2,1)S(1)}, u32[]{:S(2)}, u32[]{:S(2)}) %collective-permute-start) | collective-permute-done | bytes 4194336 | tf_op jit(solution)/shard_map/ppermute | solution.py:155
  212.7 2.0 copy-done.5
  214.6 6.7 %fusion.3 = bf16[1024,4,512]{2,0,1:T(8,128)(2,1)} fusion(bf16[1024,4,512]{2,0,1:T(8,128)(2,1)} %copy-done.5, bf16[1024,4,1,512]{3,2,1,0:T(2,128)(2,1)S(1)} %get-tuple-element.24), kind=kLoop, calls=%fused_computation.5 | loop fusion | flops 8388608 | bytes 12582912 | tf_op jit(solution)/shard_map/convert_element_type | solution.py:156
  221.4 0.3 all-gather.5.cloned.1.call-start
  221.7 1.3 copy-done.2
  223.0 9.0 %multiply_reduce_fusion.1 = (f32[1024]{0:T(1024)S(1)}, f32[512]{0:T(512)S(1)}, f32[512]{0:T(512)S(1)}, f32[1024]{0:T(1024)S(1)}, f32[512,1024]{1,0:T(8,128)}) fusion(f32[2,32,8,1,1024]{4,2,1,0,3:T(8,128)S(1)} %copy-done.2, f32[512]{0:T(512)S(1)} %div.35, f32[512]{0:T(512)S(1)} %rsqrt.12, f32[1024]{0:T(1024)S(1)} %copy-done.15, ...), kind=kOutput, calls=%fused_computation.27 | convolution fusion | flops 3225940992 | bytes 13651968 | tf_op jit(solution)/shard_map/dot_general | solution.py:41
  232.0 0.6 maximum_bitcast_fusion
  232.6 2.3 multiply_convert_fusion.1
  234.9 2.0 copy.129
  237.0 4.8 %all-to-all-start.2 = ((bf16[2,256,1,1024]{3,0,2,1:T(2,128)(2,1)}), bf16[2,256,1,1024]{3,0,2,1:T(2,128)(2,1)}, u32[]{:S(2)}, u32[]{:S(2)}) async-start(bf16[2,256,1,1024]{3,0,2,1:T(2,128)(2,1)} %copy.129), calls=%async_computation.2 | async-start | bytes 2097152 | tf_op jit(solution)/shard_map/all_to_all | solution.py:133
  241.9 36.5 %reduce-scatter.4.cloned.1.call-done = bf16[256,4,512]{2,0,1:T(8,128)(2,1)} async-done(((bf16[1024,4,512]{2,0,1:T(8,128)(2,1)}), bf16[256,4,512]{2,0,1:T(8,128)(2,1)}) %reduce-scatter.4.cloned.1.call-update) | async-done | bytes 1048592 | tf_op jit(solution)/shard_map/reduce_scatter | solution.py:157
  278.4 2.2 fusion.20
  280.6 1.5 copy.137
  282.2 74.1 %all-gather.5.cloned.1.call-done = f32[256,2,1024]{2,1,0:T(2,128)} async-done(((f32[1,2,1024]{2,1,0:T(2,128)}), f32[256,2,1024]{2,1,0:T(2,128)}) %all-gather.5.cloned.1.call-update) | async-done | bytes 2097168 | tf_op jit(solution)/shard_map/all_gather | solution.py:19
  356.3 2.2 reduce_sum.89
  358.6 0.5 slice_bitcast_fusion
  359.1 19.1 %reduce-scatter.8.cloned.1.call-done = bf16[32,1,512]{2,0,1:T(8,128)(2,1)} async-done(((bf16[32,4,512]{2,0,1:T(8,128)(2,1)}), bf16[32,1,512]{2,0,1:T(8,128)(2,1)}) %reduce-scatter.8.cloned.1.call-update) | async-done | bytes 32784 | tf_op jit(solution)/shard_map/reduce_scatter | solution.py:159
  378.2 15.8 %all-gather = bf16[32,1,4096]{2,0,1:T(8,128)(2,1)S(1)} all-gather(bf16[32,1,512]{2,0,1:T(8,128)(2,1)} %reduce-scatter.8.cloned.1.call-done), channel_id=2, replica_groups=mesh['x'=4,'core'=2,'y'=4,'z'=8] {'x','core'}, dimensions={2}, use_global_device_ids=true | all-gather | bytes 294912 | tf_op jit(solution)/shard_map/all_gather | solution.py:160
  394.1 0.8 slice.31
  394.8 0.7 slice.32
  (71 shorter events, 3.0 us)
Async XLA Ops:
  8.0 75.8 %copy-start = (bf16[1024,1024]{1,0:T(8,128)(2,1)S(1)}, bf16[1024,1024]{1,0:T(8,128)(2,1)}, u32[]{:S(2)}) copy-start(bf16[1024,1024]{1,0:T(8,128)(2,1)} %param.17) | copy-start | bytes 6291460
  8.0 18.6 %copy-start.17 = (s32[2,4,3]{1,0,2:T(2,128)S(1)}, s32[2,4,3]{1,0,2:T(2,128)}, u32[]{:S(2)}) copy-start(s32[2,4,3]{1,0,2:T(2,128)} %param.12) | copy-start | bytes 292
  8.0 18.6 %copy-start.18 = (s32[2,4]{1,0:T(2,128)S(1)}, s32[2,4]{1,0:T(2,128)}, u32[]{:S(2)}) copy-start(s32[2,4]{1,0:T(2,128)} %param.13) | copy-start | bytes 100
  11.0 36.9 %all-to-all-start = ((bf16[2,8,32,1024]{3,1,0,2:T(8,128)(2,1)}), bf16[2,8,32,1024]{3,1,0,2:T(8,128)(2,1)S(1)}, u32[]{:S(2)}, u32[]{:S(2)}) async-start(bf16[2,8,32,1024]{3,1,0,2:T(8,128)(2,1)} %copy.100), calls=%async_computation | async-start | bytes 2097152 | tf_op jit(solution)/shard_map/all_to_all | solution.py:63
  47.9 33.6 %all-to-all-start.1 = ((bf16[2,8,32,1024]{3,1,0,2:T(8,128)(2,1)}), bf16[2,8,32,1024]{3,1,0,2:T(8,128)(2,1)}, u32[]{:S(2)}, u32[]{:S(2)}) async-start(bf16[2,8,32,1024]{3,1,0,2:T(8,128)(2,1)} %copy.114), calls=%async_computation.1 | async-start | bytes 2097152 | tf_op jit(solution)/shard_map/all_to_all | solution.py:64
  56.3 222.0 %reduce-scatter.4.cloned.1.call-start = ((), (), s32[]{:S(2)}) async-start(), calls=%async_computation.6 | async-start | bytes 5242880 | tf_op jit(solution)/shard_map/reduce_scatter | solution.py:157
  56.7 5.8 %copy-start.15 = (f32[1024]{0:T(1024)S(1)}, f32[1024]{0:T(1024)}, u32[]{:S(2)}) copy-start(f32[1024]{0:T(1024)} %param.14) | copy-start | bytes 12292
  56.7 5.8 %copy-start.16 = (f32[1024]{0:T(1024)S(1)}, f32[1024]{0:T(1024)}, u32[]{:S(2)}) copy-start(f32[1024]{0:T(1024)} %param.15) | copy-start | bytes 12292
  64.5 7.0 %copy-start.8 = (bf16[512,1024]{1,0:T(8,128)(2,1)}, bf16[512,1024]{1,0:T(8,128)(2,1)S(1)}, u32[]{:S(2)}) copy-start(bf16[512,1024]{1,0:T(8,128)(2,1)S(1)} %add_convert_fusion) | copy-start | bytes 3145732
  82.8 1.0 copy-start.10
  99.1 5.9 %copy-start.6 = (bf16[2,256,16,64]{1,3,2,0:T(8,128)(2,1)S(1)}, bf16[2,256,16,64]{1,3,2,0:T(8,128)(2,1)}, u32[]{:S(2)}) copy-start(bf16[2,256,16,64]{1,3,2,0:T(8,128)(2,1)} %copy.120) | copy-start | bytes 3145732
  99.1 5.9 %copy-start.7 = (bf16[2,256,16,64]{1,3,2,0:T(8,128)(2,1)S(1)}, bf16[2,256,16,64]{1,3,2,0:T(8,128)(2,1)}, u32[]{:S(2)}) copy-start(bf16[2,256,16,64]{1,3,2,0:T(8,128)(2,1)} %copy.112) | copy-start | bytes 3145732
  138.0 4.9 %copy-start.3 = (bf16[2,256,16,64]{1,3,2,0:T(8,128)(2,1)S(1)}, bf16[2,256,16,64]{1,3,2,0:T(8,128)(2,1)}, u32[]{:S(2)}) copy-start(bf16[2,256,16,64]{1,3,2,0:T(8,128)(2,1)} %copy.119) | copy-start | bytes 3145732
  138.0 6.1 %copy-start.19 = (f32[2,16,256,256]{2,3,1,0:T(8,128)S(1)}, f32[2,16,256,256]{2,3,1,0:T(8,128)}, u32[]{:S(2)}) copy-start(f32[2,16,256,256]{2,3,1,0:T(8,128)} %get-tuple-element.32) | copy-start | bytes 25165828
  144.1 1.2 copy-start.13
  145.4 1.4 copy-start.12
  148.1 2.7 copy-start.11
  152.1 1.2 copy-start.9
  153.3 3.5 copy-start.14
  201.3 11.4 %collective-permute-start = (bf16[1024,4,512]{2,0,1:T(8,128)(2,1)S(1)}, bf16[1024,4,512]{2,0,1:T(8,128)(2,1)S(1)}, u32[]{:S(2)}, u32[]{:S(2)}) collective-permute-start(bf16[1024,4,512]{2,0,1:T(8,128)(2,1)S(1)} %bitcast.122), channel_id=1, source_target_pairs={{0,32},{32,0},{1,33},{33,1},{2,34},{34,2},{3,35},{35,3},{4,36},{36... | collective-permute-start | bytes 12582920 | tf_op jit(solution)/shard_map/ppermute | solution.py:155
  212.7 2.0 copy-start.5
  221.4 1.6 copy-start.2
  221.4 134.9 %all-gather.5.cloned.1.call-start = ((), (), s32[]{:S(2)}) async-start(), calls=%async_computation.9 | async-start | bytes 2105344 | tf_op jit(solution)/shard_map/all_gather | solution.py:19
  232.6 45.8 %copy-start.4 = (bf16[2,8,32,1024]{3,2,1,0:T(8,128)(2,1)S(1)}, bf16[2,8,32,1024]{3,2,1,0:T(8,128)(2,1)}, u32[]{:S(2)}) copy-start(bf16[2,8,32,1024]{3,2,1,0:T(8,128)(2,1)} %param.10) | copy-start | bytes 3145732
  237.0 41.5 %all-to-all-start.2 = ((bf16[2,256,1,1024]{3,0,2,1:T(2,128)(2,1)}), bf16[2,256,1,1024]{3,0,2,1:T(2,128)(2,1)}, u32[]{:S(2)}, u32[]{:S(2)}) async-start(bf16[2,256,1,1024]{3,0,2,1:T(2,128)(2,1)} %copy.129), calls=%async_computation.2 | async-start | bytes 2097152 | tf_op jit(solution)/shard_map/all_to_all | solution.py:133
  241.8 116.7 %reduce-scatter.6.cloned.1.call-start = ((), (), s32[]{:S(2)}) async-start(), calls=%async_computation.7 | async-start | bytes 1179648 | tf_op jit(solution)/shard_map/reduce_scatter | solution.py:158
  278.4 99.8 %reduce-scatter.8.cloned.1.call-start = ((), (), s32[]{:S(2)}) async-start(), calls=%async_computation.8 | async-start | bytes 163840 | tf_op jit(solution)/shard_map/reduce_scatter | solution.py:159
  278.4 117.1 %copy-start.1 = (bf16[1024,1024]{1,0:T(8,128)(2,1)S(1)}, bf16[1024,1024]{1,0:T(8,128)(2,1)}, u32[]{:S(2)}) copy-start(bf16[1024,1024]{1,0:T(8,128)(2,1)} %param.17) | copy-start | bytes 6291460
Sparse Core Ops, SparseCore 0:
  221.5 56.7 reduce-scatter.3
  280.9 34.5 reduce-scatter.5
  358.7 19.4 reduce-scatter.7
Sparse Core Ops, SparseCore 1:
  232.7 123.5 all-gather.4
